TPU v7x, 128 devices: a whole 4x4x4 slice. The times are simulated.
128 devices in a mesh: dp: 32 (over y, z_lo, x), tensor: 4 (over z_hi, core).
Axes of the slice: x: 4, y: 4, z: 4 (z_hi: 2, z_lo: 2; z = z_hi * 2 + z_lo), core: 2. Of those that a mesh axis runs over, the one named last changes fastest.
Arguments:
- tokens: bfloat16 [32768, 4096], P('dp'), may hold values from -6 to 6
- grad_out: bfloat16 [32768, 2048], P('dp', 'tensor'), may hold values from -12 to 12
- w_query: bfloat16 [4096, 2048], P('dp', 'tensor'), may hold values from -2 to 2
- w_key: bfloat16 [4096, 512], P('dp', 'tensor'), may hold values from -2 to 2
- value_matrix: bfloat16 [4096, 512], P('dp', 'tensor'), may hold values from -0.09375 to 0.09375
Outputs:
- grad_tokens: bfloat16 [32768, 4096], P('dp', 'tensor')
- grad_query: bfloat16 [4096, 2048], P('dp', 'tensor')
- grad_key: bfloat16 [4096, 512], P('dp', 'tensor')
- grad_value: bfloat16 [4096, 512], P('dp', 'tensor')
All inputs are finite; a program needn't handle non-finite values.
Results may differ from a plain program's by a relative error of at most 0.03.
The roundings to bfloat16 on the way count: a program that leaves them out, or rounds other values in their place, can miss the bound.
Values may be sent and summed in bfloat16 or wider, within the bound.
No kernel may reach another device: no remote copies, remote signals or barrier semaphores. Data moves between devices by JAX's collectives and lax.ppermute only.
A program may use at most 192 MiB of HBM per device.

v0:
```python
import jax
import jax.numpy as jnp
from jax import lax
from jax.sharding import Mesh
from jax.sharding import PartitionSpec as P

MODEL_WIDTH = 4096
HEAD_SIZE = 128
rope_base = 500000.0


def position_tables(length, head_dim):
    half_dim = head_dim // 2
    positions = jnp.arange(length, dtype=jnp.float32)
    inverse = jnp.power(
        jnp.float32(rope_base), -2.0 * jnp.arange(half_dim, dtype=jnp.float32) / head_dim
    )
    angles = positions[:, None] * inverse[None, :]
    cosine = jnp.concatenate([jnp.cos(angles), jnp.cos(angles)], axis=-1)[:, None, :]
    sine_table = jnp.concatenate([jnp.sin(angles), jnp.sin(angles)], axis=-1)[:, None, :]
    return (cosine, sine_table)


def half_turn(values):
    lower, upper = jnp.split(values, 2, axis=-1)
    return jnp.concatenate([-upper, lower], axis=-1)


def rotate_forward(values, cosine, sine_table):
    return values * cosine + half_turn(values) * sine_table


def rotate_back(grads, cosine, sine_table):
    return grads * cosine - half_turn(grads * sine_table)


def attention_backward(unrotated_query, unrotated_key, projected_value, upstream_flat, kv_heads):
    length = unrotated_query.shape[0]
    heads = unrotated_query.shape[1] // HEAD_SIZE
    group_size = heads // kv_heads
    cosine, sine_table = position_tables(length, HEAD_SIZE)
    query = rotate_forward(
        unrotated_query.reshape(length, heads, HEAD_SIZE), cosine, sine_table
    ).astype(jnp.bfloat16)
    key = rotate_forward(
        unrotated_key.reshape(length, kv_heads, HEAD_SIZE), cosine, sine_table
    ).astype(jnp.bfloat16)
    value = projected_value.reshape(length, kv_heads, HEAD_SIZE).astype(jnp.bfloat16)
    query_grouped = query.reshape(length, kv_heads, group_size, HEAD_SIZE)
    upstream = upstream_flat.reshape(length, kv_heads, group_size, HEAD_SIZE)
    scale = 1.0 / jnp.sqrt(jnp.float32(HEAD_SIZE))
    scores = (
        jnp.einsum("ikgd,jkd->kgij", query_grouped, key, preferred_element_type=jnp.float32) * scale
    )
    positions = jnp.arange(length, dtype=jnp.int32)
    causal = positions[:, None] >= positions[None, :]
    scores = jnp.where(causal, scores, -jnp.inf)
    row_max = jnp.max(scores, axis=-1, keepdims=True)
    weights = jnp.exp(scores - row_max)
    weights = weights / jnp.sum(weights, axis=-1, keepdims=True)
    weights_b = weights.astype(jnp.bfloat16)
    dprob = jnp.einsum("ikgd,jkd->kgij", upstream, value, preferred_element_type=jnp.float32)
    rowdot = jnp.sum(weights * dprob, axis=-1, keepdims=True)
    dscore = (weights * (dprob - rowdot) * scale).astype(jnp.bfloat16)
    dquery = jnp.einsum("kgij,jkd->ikgd", dscore, key, preferred_element_type=jnp.float32).reshape(
        length, heads, HEAD_SIZE
    )
    dkey = jnp.einsum("kgij,ikgd->jkd", dscore, query_grouped, preferred_element_type=jnp.float32)
    dvalue = jnp.einsum("kgij,ikgd->jkd", weights_b, upstream, preferred_element_type=jnp.float32)
    query_gradient = (
        rotate_back(dquery, cosine, sine_table)
        .astype(jnp.bfloat16)
        .reshape(length, heads * HEAD_SIZE)
    )
    key_gradient = (
        rotate_back(dkey, cosine, sine_table)
        .astype(jnp.bfloat16)
        .reshape(length, kv_heads * HEAD_SIZE)
    )
    value_gradient = dvalue.astype(jnp.bfloat16).reshape(length, kv_heads * HEAD_SIZE)
    return (query_gradient, key_gradient, value_gradient)


DP_AXES = ("y", "zl", "x")
TP_AXES = ("zh", "c")


def gather_rows(block):
    block = lax.all_gather(block, "x", axis=0, tiled=True)
    block = lax.all_gather(block, "zl", axis=0, tiled=True)
    return lax.all_gather(block, "y", axis=0, tiled=True)


def scatter_rows(block):
    block = lax.psum_scatter(block, "y", scatter_dimension=0, tiled=True)
    block = lax.psum_scatter(block, "zl", scatter_dimension=0, tiled=True)
    return lax.psum_scatter(block, "x", scatter_dimension=0, tiled=True)


def body(tokens, grad_out, w_query, w_key, value_matrix):
    query_cols = w_query.shape[1]
    key_value_columns = w_key.shape[1]
    kv_dev = key_value_columns // HEAD_SIZE
    weights_all = gather_rows(jnp.concatenate([w_query, w_key, value_matrix], axis=1))
    projected = jnp.dot(tokens, weights_all, preferred_element_type=jnp.float32)
    unrotated_query = projected[:, :query_cols]
    unrotated_key = projected[:, query_cols : query_cols + key_value_columns]
    projected_value = projected[:, query_cols + key_value_columns :]
    query_gradient, key_gradient, value_gradient = attention_backward(
        unrotated_query, unrotated_key, projected_value, grad_out, kv_dev
    )
    combined = jnp.concatenate([query_gradient, key_gradient, value_gradient], axis=1)
    partial_sum = lax.dot_general(
        combined, weights_all, (((1,), (1,)), ((), ())), preferred_element_type=jnp.float32
    )
    grad_tokens = lax.psum_scatter(
        partial_sum.astype(jnp.bfloat16), TP_AXES, scatter_dimension=1, tiled=True
    )
    grads_all = scatter_rows(
        lax.dot_general(
            tokens, combined, (((0,), (0,)), ((), ())), preferred_element_type=jnp.float32
        ).astype(jnp.bfloat16)
    )
    grad_query = grads_all[:, :query_cols]
    grad_key = grads_all[:, query_cols : query_cols + key_value_columns]
    grad_value = grads_all[:, query_cols + key_value_columns :]
    return (grad_tokens, grad_query, grad_key, grad_value)


def solution(mesh):
    view = Mesh(mesh.devices.reshape(4, 2, 4, 2, 2), DP_AXES + TP_AXES)
    rows = P(DP_AXES, None)
    split = P(DP_AXES, TP_AXES)
    in_specs = (rows, split, split, split, split)
    out_specs = (split, split, split, split)
    return jax.shard_map(body, mesh=view, in_specs=in_specs, out_specs=out_specs, check_vma=False)
```

profile of v0, /device:TPU:1, one launch (start us, length us, event | category | flops | bytes accessed | tf_op | source)
XLA Modules:
  0.0 409.0 jit_solution(8105089729358219273)
XLA Ops:
  8.2 13.3 %all_gather.9 = bf16[512,768]{1,0:T(8,128)(2,1)} all-gather(bf16[128,768]{1,0:T(8,128)(2,1)S(1)} %pad_maximum_fusion.6), channel_id=1, replica_groups=mesh['y'=4,'zl'=2,'x'=4,'zh'=2,'c'=2] {'x'}, dimensions={0}, use_global_device_ids=true | all-gather | bytes 983040 | tf_op jit(solution)/shard_map/all_gather | solution.py:89
  21.6 34.3 %all-gather.3.cloned.1.call-done = bf16[1024,768]{1,0:T(8,128)(2,1)} async-done(((bf16[512,768]{1,0:T(8,128)(2,1)}), bf16[1024,768]{1,0:T(8,128)(2,1)}) %all-gather.3.cloned.1.call-update) | async-done | bytes 1572880 | tf_op jit(solution)/shard_map/all_gather | solution.py:90
  55.9 2.3 copy.44
  59.5 64.7 %all-gather.5.cloned.1.call-done = bf16[4096,768]{1,0:T(8,128)(2,1)} async-done(((bf16[1024,768]{1,0:T(8,128)(2,1)}), bf16[4096,768]{1,0:T(8,128)(2,1)}) %all-gather.5.cloned.1.call-update) | async-done | bytes 6291472 | tf_op jit(solution)/shard_map/all_gather | solution.py:91
  124.2 11.0 %convolution_bitcast_fusion = f32[1024,768]{0,1:T(8,128)S(1)} fusion(bf16[4096,768]{1,0:T(8,128)(2,1)} %all-gather.5.cloned.1.call-done, bf16[1024,4096]{1,0:T(8,128)(2,1)} %param.5), kind=kOutput, calls=%fused_computation.29 | convolution fusion | flops 6442450944 | bytes 17825792 | tf_op jit(solution)/shard_map/dot_general | solution.py:105
  135.3 1.6 slice.26
  136.9 1.8 slice_negate_fusion.1
  141.0 3.1 fusion.6
  144.1 3.7 fusion.5
  148.4 6.0 %fusion.20 = bf16[1024,128]{0,1:T(8,128)(2,1)} fusion(bf16[1024,4,128]{0,2,1:T(8,128)(2,1)S(1)} %bitcast.123, f32[4,1024]{1,0:T(4,128)S(1)} %fusion.5, f32[4,1024]{1,0:T(4,128)S(1)} %get-tuple-element.27, f32[1024,1024,4]{1,0,2:T(8,128)S(1)} %get-tuple-element.28, pred[1024,1024]{0,1:T(8,128)(4,1)S(1)} %iota_compare_fusion), kind=kOutput, calls=%fused_computation.33 | convolution fusion | flops 1094844416 | bytes 19169280 | tf_op jit(solution)/shard_map/kgij,ikgd->jkd/dot_general | solution.py:69
  154.4 11.1 %fusion = (f32[4,1024]{1,0:T(4,128)}, f32[1024,1024,4]{1,0,2:T(8,128)}) fusion(f32[4,1024]{1,0:T(4,128)} %copy-done.14, f32[4,1024]{1,0:T(4,128)} %copy-done.13, f32[1024,1024,4]{1,0,2:T(8,128)S(1)} %get-tuple-element.28, pred[1024,1024]{0,1:T(8,128)(4,1)S(1)} %iota_compare_fusion, bf16[1024,4,128]{0,2,1:T(8,128)(2,1)} %bitcast.122, f32[1024,768]{0,1:T(8,128)} %copy-done.2), kind=kOutput, calls=%fused_computation.3 | convolution fusion | flops 1098903552 | bytes 35962880 | tf_op jit(solution)/shard_map/ikgd,jkd->kgij/dot_general | solution.py:62
  165.5 11.6 %fusion.7 = bf16[4,1024,1024]{1,2,0:T(8,128)(2,1)} fusion(f32[1024,1024,4]{1,0,2:T(8,128)} %get-tuple-element.30, f32[4,1024]{1,0:T(4,128)} %get-tuple-element.29, f32[4,1024]{1,0:T(4,128)} %copy-done.14, f32[4,1024]{1,0:T(4,128)} %copy-done.13, f32[1024,1024,4]{1,0,2:T(8,128)S(1)} %get-tuple-element.28, pred[1024,1024]{0,1:T(8,128)(4,1)S(1)} %iota_compare_fusion), kind=kLoop, calls=%fused_computation.11 | loop fusion | flops 33554432 | bytes 43040768 | tf_op jit(solution)/shard_map/reshape.19
  177.1 7.8 %bitcast_multiply_fusion.4 = (f32[1024,1,128]{0,2,1:T(8,128)S(1)}, f32[1024,1,128]{0,2,1:T(8,128)S(1)}) fusion(f32[1024,64]{0,1:T(8,128)} %copy-done.7, bf16[4,1024,1024]{1,2,0:T(8,128)(2,1)} %fusion.7, f32[1024,4,128]{0,2,1:T(8,128)} %copy-done.1, f32[1024,4,128]{0,2,1:T(8,128)} %bitcast.7, f32[1024,128]{0,1:T(8,128)} %copy-done.3), kind=kOutput, calls=%fused_computation.45 | convolution fusion | flops 1075576832 | bytes 14417920 | tf_op jit(solution)/shard_map/kgij,ikgd->jkd/dot_general | solution.py:68
  185.0 1.4 bitcast_multiply_fusion.3
  188.9 1.3 slice-done.1
  190.2 8.7 %fusion.11 = bf16[4096,768]{0,1:T(8,128)(2,1)} fusion(bf16[1024,4096]{1,0:T(8,128)(2,1)S(1)} %bitcast.125, bf16[1024,128]{0,1:T(8,128)(2,1)S(1)} %copy-done.15, bf16[1024,128]{0,1:T(8,128)(2,1)S(1)} %fusion.27, bf16[1024,512]{0,1:T(8,128)(2,1)S(1)} %fusion.16), kind=kOutput, calls=%fused_computation.17 | convolution fusion | flops 6450315264 | bytes 16252928 | tf_op jit(solution)/shard_map/dot_general | solution.py:120
  199.0 64.8 %reduce-scatter.9.cloned.1.call-done = bf16[1024,768]{0,1:T(8,128)(2,1)} async-done(((bf16[4096,768]{0,1:T(8,128)(2,1)}), bf16[1024,768]{0,1:T(8,128)(2,1)}) %reduce-scatter.9.cloned.1.call-update) | async-done | bytes 1572880 | tf_op jit(solution)/shard_map/reduce_scatter | solution.py:95
  263.8 30.5 %reduce-scatter.11.cloned.1.call-done = bf16[512,768]{0,1:T(8,128)(2,1)} async-done(((bf16[1024,768]{0,1:T(8,128)(2,1)}), bf16[512,768]{0,1:T(8,128)(2,1)}) %reduce-scatter.11.cloned.1.call-update) | async-done | bytes 786448 | tf_op jit(solution)/shard_map/reduce_scatter | solution.py:96
  294.3 2.4 copy.39
  296.8 11.8 %convolution_convert_fusion = bf16[1024,4096]{1,0:T(8,128)(2,1)} fusion(bf16[4096,768]{1,0:T(8,128)(2,1)} %all-gather.5.cloned.1.call-done, bf16[1024,128]{0,1:T(8,128)(2,1)S(1)} %copy-done.15, bf16[1024,128]{0,1:T(8,128)(2,1)S(1)} %fusion.27, bf16[1024,512]{0,1:T(8,128)(2,1)S(1)} %fusion.16), kind=kOutput, calls=%fused_computation.15 | convolution fusion | flops 6451363840 | bytes 16252928 | tf_op jit(solution)/shard_map/dot_general | solution.py:113
  308.6 10.5 %reduce-scatter.13.cloned.1.call-done = bf16[128,768]{1,0:T(8,128)(2,1)} async-done(((bf16[512,768]{1,0:T(8,128)(2,1)}), bf16[128,768]{1,0:T(8,128)(2,1)}) %reduce-scatter.13.cloned.1.call-update) | async-done | bytes 196624
  319.2 1.6 slice.28
  320.7 1.4 fusion.39
  322.2 80.0 %reduce-scatter.7.cloned.1.call-done = bf16[1024,1024]{1,0:T(8,128)(2,1)} async-done(((bf16[1024,4096]{1,0:T(8,128)(2,1)}), bf16[1024,1024]{1,0:T(8,128)(2,1)}) %reduce-scatter.7.cloned.1.call-update) | async-done | bytes 2097168 | tf_op jit(solution)/shard_map/reduce_scatter | solution.py:116
  (62 shorter events, 8.0 us)
Async XLA Ops:
  7.2 48.7 %all-gather.3.cloned.1.call-start = ((), (), s32[]{:S(2)}) async-start(), calls=%async_computation.4 | async-start | bytes 2359296 | tf_op jit(solution)/shard_map/all_gather | solution.py:90
  21.5 102.7 %all-gather.5.cloned.1.call-start = ((), (), s32[]{:S(2)}) async-start(), calls=%async_computation.5 | async-start | bytes 7864320 | tf_op jit(solution)/shard_map/all_gather | solution.py:91
  55.9 207.8 %reduce-scatter.9.cloned.1.call-start = ((), (), s32[]{:S(2)}) async-start(), calls=%async_computation.7 | async-start | bytes 7864320 | tf_op jit(solution)/shard_map/reduce_scatter | solution.py:95
  59.5 79.2 %copy-start.7 = (f32[1024,64]{0,1:T(8,128)}, f32[1024,64]{0,1:T(8,128)S(1)}, u32[]{:S(2)}) copy-start(f32[1024,64]{0,1:T(8,128)S(1)} %get-tuple-element.26) | copy-start | bytes 786436
  59.5 79.2 %copy-start.10 = (f32[1024,64]{0,1:T(8,128)}, f32[1024,64]{0,1:T(8,128)S(1)}, u32[]{:S(2)}) copy-start(f32[1024,64]{0,1:T(8,128)S(1)} %get-tuple-element.25) | copy-start | bytes 786436
  135.2 4.4 %copy-start.2 = (f32[1024,768]{0,1:T(8,128)}, f32[1024,768]{0,1:T(8,128)S(1)}, u32[]{:S(2)}) copy-start(f32[1024,768]{0,1:T(8,128)S(1)} %convolution_bitcast_fusion) | copy-start | bytes 9437188
  138.9 0.8 copy-start.5
  138.9 1.4 copy-start.3
  138.9 5.2 %copy-start.8 = (bf16[1024,128,1]{0,1,2:T(8,128)(2,1)}, bf16[1024,128,1]{0,1,2:T(8,128)(2,1)S(1)}, u32[]{:S(2)}) copy-start(bf16[1024,128,1]{0,1,2:T(8,128)(2,1)S(1)} %get-tuple-element.21) | copy-start | bytes 786436
  139.7 1.3 copy-start.1
  144.1 3.7 copy-start.13
  144.1 4.3 %copy-start.12 = (bf16[1024,512]{0,1:T(8,128)(2,1)S(1)}, bf16[1024,512]{0,1:T(8,128)(2,1)}, u32[]{:S(2)}) copy-start(bf16[1024,512]{0,1:T(8,128)(2,1)} %copy.44) | copy-start | bytes 3145732
  147.8 0.6 copy-start.14
  177.1 7.9 %copy-start = (bf16[4,1024,1024]{1,2,0:T(8,128)(2,1)S(1)}, bf16[4,1024,1024]{1,2,0:T(8,128)(2,1)}, u32[]{:S(2)}) copy-start(bf16[4,1024,1024]{1,2,0:T(8,128)(2,1)} %fusion.7) | copy-start | bytes 25165828
  177.1 7.9 %copy-start.6 = (f32[1024,128]{0,1:T(8,128)S(1)}, f32[1024,128]{0,1:T(8,128)}, u32[]{:S(2)}) copy-start(f32[1024,128]{0,1:T(8,128)} %copy-done.5) | copy-start | bytes 1572868
  177.1 7.9 %copy-start.9 = (bf16[1024,128,1]{0,1,2:T(8,128)(2,1)S(1)}, bf16[1024,128,1]{0,1,2:T(8,128)(2,1)}, u32[]{:S(2)}) copy-start(bf16[1024,128,1]{0,1,2:T(8,128)(2,1)} %copy-done.8) | copy-start | bytes 786436
  186.4 1.0 copy-start.4
  186.4 1.6 copy-start.11
  186.4 2.4 slice-start
  186.6 2.3 copy-start.15
  186.6 3.6 slice-start.1
  198.9 95.4 %reduce-scatter.11.cloned.1.call-start = ((), (), s32[]{:S(2)}) async-start(), calls=%async_computation.8 | async-start | bytes 2359296 | tf_op jit(solution)/shard_map/reduce_scatter | solution.py:96
  263.8 55.4 %reduce-scatter.13.cloned.1.call-start = ((), (), s32[]{:S(2)}) async-start(), calls=%async_computation.9 | async-start | bytes 983040
  296.7 105.4 %reduce-scatter.7.cloned.1.call-start = ((), (), s32[]{:S(2)}) async-start(), calls=%async_computation.6 | async-start | bytes 10485760 | tf_op jit(solution)/shard_map/reduce_scatter | solution.py:116
Sparse Core Ops, SparseCore 0:
  21.6 34.1 all-gather.2
  57.5 66.6 all-gather.4
  199.0 64.6 reduce-scatter.8
  265.9 28.3 reduce-scatter.10
  296.8 22.2 reduce-scatter.12
  322.5 79.5 reduce-scatter.6
where the time goes:
time: 409 us
  waiting for transfers between devices  285 us (70%)
  matrix products  60.9 us (15%)
  other arithmetic  21.5 us (5%)
  between operations  14.4 us (4%)
  local copies, waits for them, and re-layouts  13.7 us (3%)
  blocking collectives  13.3 us (3%)
    reduce_scatter x1, waiting for transfers between devices, body(): lax.psum_scatter(partial_sum.astype(jnp.bfloat16), TP_AXES, scatter_dimen...  80 us
    reduce_scatter x1, waiting for transfers between devices, scatter_rows(): block = lax.psum_scatter(block, 'y', scatter_dimension=0, tiled=True)  64.8 us
    all_gather x1, waiting for transfers between devices, gather_rows(): return lax.all_gather(block, 'y', axis=0, tiled=True)  64.7 us
    all_gather x1, waiting for transfers between devices, gather_rows(): block = lax.all_gather(block, 'zl', axis=0, tiled=True)  34.3 us
    reduce_scatter x1, waiting for transfers between devices, scatter_rows(): block = lax.psum_scatter(block, 'zl', scatter_dimension=0, tiled=True)  30.5 us
    all_gather x1, blocking collectives, gather_rows(): block = lax.all_gather(block, 'x', axis=0, tiled=True)  13.3 us
    dot_general x1, matrix products, body(): lax.dot_general(combined, weights_all, (((1,), (1,)), ((), ())), preferre...  11.8 us
    another operation x1, other arithmetic  11.6 us
  transfers between devices with their start and end apart: 6, of which 6 were waited for; matrix products, arithmetic and copies ran while one was open for 4% of the time, Pallas kernels for 0%

commit v1 on v0

--- a/solution.py
+++ b/solution.py
@@ -7,6 +7,11 @@
 MODEL_WIDTH = 4096
 HEAD_SIZE = 128
 rope_base = 500000.0
+
+
+def swapped_in(x, axis, along):
+    stack = jnp.stack([x] * lax.axis_size(axis))
+    return jnp.concatenate(lax.all_to_all(stack, axis, 0, 0), axis=along)
 
 
 def position_tables(length, head_dim):
@@ -87,7 +92,7 @@
 
 def gather_rows(block):
     block = lax.all_gather(block, "x", axis=0, tiled=True)
-    block = lax.all_gather(block, "zl", axis=0, tiled=True)
+    block = swapped_in(block, "zl", 0)
     return lax.all_gather(block, "y", axis=0, tiled=True)
 
 

time: 409 us -> 396 us (0.968)
  waiting for transfers between devices: 285 us -> 252 us
  blocking collectives: 13.3 us -> 33.7 us
    all_gather x1 -> x0, waiting for transfers between devices: 34.3 us -> none  [gather_rows(): block = lax.all_gather(block, 'zl', axis=0, tiled=True)]
    all_to_all x0 -> x1, blocking collectives: none -> 20.8 us  [swapped_in(): return jnp.concatenate(lax.all_to_all(stack, axis, 0, 0), axis=along)]
    another operation x1 -> x2, other arithmetic: 11.6 us -> 11.7 us
    unnamed x7 -> x6, waiting for transfers between devices: 10.6 us -> 10.6 us
  transfers between devices with their start and end apart: 6 -> 5, of which waited for: 6 -> 5; matrix products, arithmetic and copies ran while one was open for 4% -> 4% of each run, Pallas kernels for 0% -> 0%
where the time goes in v1:
time: 396 us; the launch traced here: 395 us
  waiting for transfers between devices  252 us (64%)
  matrix products  60.9 us (15%)
  blocking collectives  33.7 us (9%)
  other arithmetic  21.7 us (5%)
  between operations  14.1 us (4%)
  local copies, waits for them, and re-layouts  12.7 us (3%)
    reduce_scatter x1, waiting for transfers between devices, body(): lax.psum_scatter(partial_sum.astype(jnp.bfloat16), TP_AXES, scatter_dimen...  80 us
    all_gather x1, waiting for transfers between devices, gather_rows(): return lax.all_gather(block, 'y', axis=0, tiled=True)  66 us
    reduce_scatter x1, waiting for transfers between devices, scatter_rows(): block = lax.psum_scatter(block, 'y', scatter_dimension=0, tiled=True)  64.8 us
    reduce_scatter x1, waiting for transfers between devices, scatter_rows(): block = lax.psum_scatter(block, 'zl', scatter_dimension=0, tiled=True)  30.6 us
    all_to_all x1, blocking collectives, swapped_in(): return jnp.concatenate(lax.all_to_all(stack, axis, 0, 0), axis=along)  20.8 us
    all_gather x1, blocking collectives, gather_rows(): block = lax.all_gather(block, 'x', axis=0, tiled=True)  12.9 us
    dot_general x1, matrix products, body(): lax.dot_general(combined, weights_all, (((1,), (1,)), ((), ())), preferre...  11.8 us
    another operation x1, other arithmetic  11.6 us
  transfers between devices with their start and end apart: 5, of which 5 were waited for; matrix products, arithmetic and copies ran while one was open for 4% of the time, Pallas kernels for 0%

profile of v1, /device:TPU:1, one launch (start us, length us, event | category | flops | bytes accessed | tf_op | source)
XLA Modules:
  0.0 395.5 jit_solution(3762333005702257613)
XLA Ops:
  8.3 12.9 %all_gather.6 = bf16[512,768]{1,0:T(8,128)(2,1)S(1)} all-gather(bf16[128,768]{1,0:T(8,128)(2,1)S(1)} %pad_maximum_fusion.7), channel_id=1, replica_groups=mesh['y'=4,'zl'=2,'x'=4,'zh'=2,'c'=2] {'x'}, dimensions={0}, use_global_device_ids=true | all-gather | bytes 983040 | tf_op jit(solution)/shard_map/all_gather | solution.py:94
  21.3 20.8 %all_to_all.5 = bf16[2,512,768]{2,1,0:T(8,128)(2,1)} all-to-all(bf16[2,512,768]{2,1,0:T(8,128)(2,1)S(1)} %pad_maximum_fusion.1), channel_id=1, replica_groups=mesh['y'=4,'zl'=2,'x'=4,'zh'=2,'c'=2] {'zl'}, dimensions={0} | all-to-all | bytes 3145728 | tf_op jit(solution)/shard_map/all_to_all | solution.py:14
  42.2 1.3 copy.44
  44.9 66.0 %all-gather.2.cloned.1.call-done = bf16[4096,768]{1,0:T(8,128)(2,1)} async-done(((bf16[1024,768]{1,0:T(8,128)(2,1)}), bf16[4096,768]{1,0:T(8,128)(2,1)}) %all-gather.2.cloned.1.call-update) | async-done | bytes 6291472 | tf_op jit(solution)/shard_map/all_gather | solution.py:96
  110.9 11.0 %convolution_bitcast_fusion = f32[1024,768]{0,1:T(8,128)S(1)} fusion(bf16[4096,768]{1,0:T(8,128)(2,1)} %all-gather.2.cloned.1.call-done, bf16[1024,4096]{1,0:T(8,128)(2,1)} %param.5), kind=kOutput, calls=%fused_computation.29 | convolution fusion | flops 6442450944 | bytes 17825792 | tf_op jit(solution)/shard_map/dot_general | solution.py:110
  122.0 1.6 slice.26
  123.6 1.7 slice_negate_fusion.1
  127.7 3.1 fusion.6
  130.8 3.7 fusion.5
  135.1 6.0 %fusion.20 = bf16[1024,128]{0,1:T(8,128)(2,1)} fusion(bf16[1024,4,128]{0,2,1:T(8,128)(2,1)S(1)} %bitcast.127, f32[4,1024]{1,0:T(4,128)S(1)} %fusion.5, f32[4,1024]{1,0:T(4,128)S(1)} %get-tuple-element.27, f32[1024,1024,4]{1,0,2:T(8,128)S(1)} %get-tuple-element.28, pred[1024,1024]{0,1:T(8,128)(4,1)S(1)} %iota_compare_fusion), kind=kOutput, calls=%fused_computation.34 | convolution fusion | flops 1094844416 | bytes 19169280 | tf_op jit(solution)/shard_map/kgij,ikgd->jkd/dot_general | solution.py:74
  141.1 11.1 %fusion = (f32[4,1024]{1,0:T(4,128)}, f32[1024,1024,4]{1,0,2:T(8,128)}) fusion(f32[4,1024]{1,0:T(4,128)} %copy-done.15, f32[4,1024]{1,0:T(4,128)} %copy-done.14, f32[1024,1024,4]{1,0,2:T(8,128)S(1)} %get-tuple-element.28, pred[1024,1024]{0,1:T(8,128)(4,1)S(1)} %iota_compare_fusion, bf16[1024,4,128]{0,2,1:T(8,128)(2,1)} %bitcast.126, f32[1024,768]{0,1:T(8,128)} %copy-done.2), kind=kOutput, calls=%fused_computation.3 | convolution fusion | flops 1098903552 | bytes 35962880 | tf_op jit(solution)/shard_map/ikgd,jkd->kgij/dot_general | solution.py:67
  152.2 11.6 %fusion.7 = bf16[4,1024,1024]{1,2,0:T(8,128)(2,1)} fusion(f32[1024,1024,4]{1,0,2:T(8,128)} %get-tuple-element.30, f32[4,1024]{1,0:T(4,128)} %get-tuple-element.29, f32[4,1024]{1,0:T(4,128)} %copy-done.15, f32[4,1024]{1,0:T(4,128)} %copy-done.14, f32[1024,1024,4]{1,0,2:T(8,128)S(1)} %get-tuple-element.28, pred[1024,1024]{0,1:T(8,128)(4,1)S(1)} %iota_compare_fusion), kind=kLoop, calls=%fused_computation.11 | loop fusion | flops 33554432 | bytes 43040768 | tf_op jit(solution)/shard_map/reshape.20
  163.8 7.8 %bitcast_multiply_fusion.4 = (f32[1024,1,128]{0,2,1:T(8,128)S(1)}, f32[1024,1,128]{0,2,1:T(8,128)S(1)}) fusion(f32[1024,64]{0,1:T(8,128)} %copy-done.7, bf16[4,1024,1024]{1,2,0:T(8,128)(2,1)} %fusion.7, f32[1024,4,128]{0,2,1:T(8,128)} %copy-done.1, f32[1024,4,128]{0,2,1:T(8,128)} %bitcast.9, f32[1024,128]{0,1:T(8,128)} %copy-done.3), kind=kOutput, calls=%fused_computation.46 | convolution fusion | flops 1075576832 | bytes 14417920 | tf_op jit(solution)/shard_map/kgij,ikgd->jkd/dot_general | solution.py:73
  171.6 1.4 bitcast_multiply_fusion.3
  175.5 1.3 slice-done.1
  176.8 8.7 %fusion.11 = bf16[4096,768]{0,1:T(8,128)(2,1)} fusion(bf16[1024,4096]{1,0:T(8,128)(2,1)S(1)} %bitcast.129, bf16[1024,128]{0,1:T(8,128)(2,1)S(1)} %copy-done.16, bf16[1024,128]{0,1:T(8,128)(2,1)S(1)} %fusion.27, bf16[1024,512]{0,1:T(8,128)(2,1)S(1)} %fusion.16), kind=kOutput, calls=%fused_computation.17 | convolution fusion | flops 6450315264 | bytes 16252928 | tf_op jit(solution)/shard_map/dot_general | solution.py:125
  185.6 64.8 %reduce-scatter.9.cloned.1.call-done = bf16[1024,768]{0,1:T(8,128)(2,1)} async-done(((bf16[4096,768]{0,1:T(8,128)(2,1)}), bf16[1024,768]{0,1:T(8,128)(2,1)}) %reduce-scatter.9.cloned.1.call-update) | async-done | bytes 1572880 | tf_op jit(solution)/shard_map/reduce_scatter | solution.py:100
  250.5 30.6 %reduce-scatter.11.cloned.1.call-done = bf16[512,768]{0,1:T(8,128)(2,1)} async-done(((bf16[1024,768]{0,1:T(8,128)(2,1)}), bf16[512,768]{0,1:T(8,128)(2,1)}) %reduce-scatter.11.cloned.1.call-update) | async-done | bytes 786448 | tf_op jit(solution)/shard_map/reduce_scatter | solution.py:101
  281.1 2.4 copy.39
  283.6 11.8 %convolution_convert_fusion = bf16[1024,4096]{1,0:T(8,128)(2,1)} fusion(bf16[4096,768]{1,0:T(8,128)(2,1)} %all-gather.2.cloned.1.call-done, bf16[1024,128]{0,1:T(8,128)(2,1)S(1)} %copy-done.16, bf16[1024,128]{0,1:T(8,128)(2,1)S(1)} %fusion.27, bf16[1024,512]{0,1:T(8,128)(2,1)S(1)} %fusion.16), kind=kOutput, calls=%fused_computation.15 | convolution fusion | flops 6451363840 | bytes 16252928 | tf_op jit(solution)/shard_map/dot_general | solution.py:118
  295.4 10.6 %reduce-scatter.13.cloned.1.call-done = bf16[128,768]{1,0:T(8,128)(2,1)} async-done(((bf16[512,768]{1,0:T(8,128)(2,1)}), bf16[128,768]{1,0:T(8,128)(2,1)}) %reduce-scatter.13.cloned.1.call-update) | async-done | bytes 196624
  306.0 1.6 slice.28
  307.5 1.4 fusion.39
  308.9 80.0 %reduce-scatter.7.cloned.1.call-done = bf16[1024,1024]{1,0:T(8,128)(2,1)} async-done(((bf16[1024,4096]{1,0:T(8,128)(2,1)}), bf16[1024,1024]{1,0:T(8,128)(2,1)}) %reduce-scatter.7.cloned.1.call-update) | async-done | bytes 2097168 | tf_op jit(solution)/shard_map/reduce_scatter | solution.py:121
  (63 shorter events, 8.1 us)
Async XLA Ops:
  7.2 35.1 %copy-start.12 = (bf16[1024,512]{1,0:T(8,128)(2,1)S(1)}, bf16[1024,512]{1,0:T(8,128)(2,1)}, u32[]{:S(2)}) copy-start(bf16[1024,512]{1,0:T(8,128)(2,1)} %param.6) | copy-start | bytes 3145732
  7.2 103.7 %all-gather.2.cloned.1.call-start = ((), (), s32[]{:S(2)}) async-start(), calls=%async_computation.5 | async-start | bytes 7864320 | tf_op jit(solution)/shard_map/all_gather | solution.py:96
  42.2 208.2 %reduce-scatter.9.cloned.1.call-start = ((), (), s32[]{:S(2)}) async-start(), calls=%async_computation.7 | async-start | bytes 7864320 | tf_op jit(solution)/shard_map/reduce_scatter | solution.py:100
  44.9 80.5 %copy-start.7 = (f32[1024,64]{0,1:T(8,128)}, f32[1024,64]{0,1:T(8,128)S(1)}, u32[]{:S(2)}) copy-start(f32[1024,64]{0,1:T(8,128)S(1)} %get-tuple-element.26) | copy-start | bytes 786436
  44.9 80.5 %copy-start.10 = (f32[1024,64]{0,1:T(8,128)}, f32[1024,64]{0,1:T(8,128)S(1)}, u32[]{:S(2)}) copy-start(f32[1024,64]{0,1:T(8,128)S(1)} %get-tuple-element.25) | copy-start | bytes 786436
  121.9 4.4 %copy-start.2 = (f32[1024,768]{0,1:T(8,128)}, f32[1024,768]{0,1:T(8,128)S(1)}, u32[]{:S(2)}) copy-start(f32[1024,768]{0,1:T(8,128)S(1)} %convolution_bitcast_fusion) | copy-start | bytes 9437188
  125.6 0.8 copy-start.5
  125.6 1.4 copy-start.3
  125.6 5.2 %copy-start.8 = (bf16[1024,128,1]{0,1,2:T(8,128)(2,1)}, bf16[1024,128,1]{0,1,2:T(8,128)(2,1)S(1)}, u32[]{:S(2)}) copy-start(bf16[1024,128,1]{0,1,2:T(8,128)(2,1)S(1)} %get-tuple-element.21) | copy-start | bytes 786436
  126.4 1.3 copy-start.1
  130.8 3.7 copy-start.14
  130.8 4.3 %copy-start.13 = (bf16[1024,512]{0,1:T(8,128)(2,1)S(1)}, bf16[1024,512]{0,1:T(8,128)(2,1)}, u32[]{:S(2)}) copy-start(bf16[1024,512]{0,1:T(8,128)(2,1)} %copy.44) | copy-start | bytes 3145732
  134.5 0.6 copy-start.15
  163.8 7.8 %copy-start = (bf16[4,1024,1024]{1,2,0:T(8,128)(2,1)S(1)}, bf16[4,1024,1024]{1,2,0:T(8,128)(2,1)}, u32[]{:S(2)}) copy-start(bf16[4,1024,1024]{1,2,0:T(8,128)(2,1)} %fusion.7) | copy-start | bytes 25165828
  163.8 7.9 %copy-start.6 = (f32[1024,128]{0,1:T(8,128)S(1)}, f32[1024,128]{0,1:T(8,128)}, u32[]{:S(2)}) copy-start(f32[1024,128]{0,1:T(8,128)} %copy-done.5) | copy-start | bytes 1572868
  163.8 7.9 %copy-start.9 = (bf16[1024,128,1]{0,1,2:T(8,128)(2,1)S(1)}, bf16[1024,128,1]{0,1,2:T(8,128)(2,1)}, u32[]{:S(2)}) copy-start(bf16[1024,128,1]{0,1,2:T(8,128)(2,1)} %copy-done.8) | copy-start | bytes 786436
  173.0 1.0 copy-start.4
  173.1 1.6 copy-start.11
  173.1 2.4 slice-start
  173.3 2.3 copy-start.16
  173.3 3.6 slice-start.1
  185.5 95.6 %reduce-scatter.11.cloned.1.call-start = ((), (), s32[]{:S(2)}) async-start(), calls=%async_computation.8 | async-start | bytes 2359296 | tf_op jit(solution)/shard_map/reduce_scatter | solution.py:101
  250.4 55.6 %reduce-scatter.13.cloned.1.call-start = ((), (), s32[]{:S(2)}) async-start(), calls=%async_computation.9 | async-start | bytes 983040
  283.5 105.4 %reduce-scatter.7.cloned.1.call-start = ((), (), s32[]{:S(2)}) async-start(), calls=%async_computation.6 | async-start | bytes 10485760 | tf_op jit(solution)/shard_map/reduce_scatter | solution.py:121
Sparse Core Ops, SparseCore 0:
  42.3 68.5 all-gather.1
  185.7 64.6 reduce-scatter.8
  252.7 28.3 reduce-scatter.10
  283.6 22.2 reduce-scatter.12
  309.3 79.5 reduce-scatter.6
